TPU v7x, 512 devices: a whole 4x4x16 slice. The times are simulated.
512 devices in a mesh: dp: 8 (over x_hi, y), tm: 64 (over x_lo, z, core).
Axes of the slice: x: 4 (x_hi: 2, x_lo: 2; x = x_hi * 2 + x_lo), y: 4, z: 16, core: 2. Of those that a mesh axis runs over, the one named last changes fastest.
Arguments:
- signal: bfloat16 [8, 65536, 256], P('dp', 'tm'), may hold values from -6 to 6
- cotangent: bfloat16 [8, 65536, 256], P('dp', 'tm'), may hold values from -6 to 6
- first_history_weight: bfloat16 [256, 512], replicated, may hold values from -0.25 to 0.25
- first_current_weight: bfloat16 [256, 512], replicated, may hold values from -0.25 to 0.25
- first_residual_weight: bfloat16 [256, 256], replicated, may hold values from -0.375 to 0.375
- second_history_weight: bfloat16 [256, 512], replicated, may hold values from -0.25 to 0.25
- second_current_weight: bfloat16 [256, 512], replicated, may hold values from -0.25 to 0.25
- second_residual_weight: bfloat16 [256, 256], replicated, may hold values from -0.375 to 0.375
Outputs:
- grad_signal: bfloat16 [8, 65536, 256], P('dp', 'tm')
- grad_past_one: bfloat16 [256, 512], replicated
- grad_now_one: bfloat16 [256, 512], replicated
- grad_mix_one: bfloat16 [256, 256], replicated
- grad_past_two: bfloat16 [256, 512], replicated
- grad_now_two: bfloat16 [256, 512], replicated
- grad_mix_two: bfloat16 [256, 256], replicated
All inputs are finite; a program needn't handle non-finite values.
Results may differ from a plain program's by a relative error of at most 0.0068.
Values may be sent and summed in bfloat16 or wider, within the bound.
No kernel may reach another device: no remote copies, remote signals or barrier semaphores. Data moves between devices by JAX's collectives and lax.ppermute only.
A program may use at most 64 MiB of HBM per device.

v0:
```python
import math
import jax
import jax.numpy as jnp
from jax import lax
from jax.sharding import PartitionSpec as P

FIRST_DILATION = 512
SECOND_DILATION = 8192


def shifted(value, axis, steps):
    count = lax.axis_size(axis)
    leading, last = (max(0, -steps), min(count, count - steps))
    return lax.ppermute(value, axis, [(source, source + steps) for source in range(leading, last)])


def forward_layer(input_traces, past_rows, tap_past, tap_now, mixing):
    channels = input_traces.shape[-1]
    flat_now = input_traces.reshape(-1, channels)
    flat_past = past_rows.reshape(-1, channels)
    pre_act = jnp.dot(flat_past, tap_past, preferred_element_type=jnp.float32) + jnp.dot(
        flat_now, tap_now, preferred_element_type=jnp.float32
    )
    half_width = pre_act.shape[1] // 2
    filter_part = jnp.tanh(pre_act[:, :half_width])
    gate_part = jax.nn.sigmoid(pre_act[:, half_width:])
    hidden = (filter_part * gate_part).astype(jnp.bfloat16)
    output = (
        flat_now.astype(jnp.float32) + jnp.dot(hidden, mixing, preferred_element_type=jnp.float32)
    ).astype(jnp.bfloat16)
    return (filter_part, gate_part, hidden, output.reshape(input_traces.shape))


def backward_layer(input_traces, past_rows, saved, incoming_gradient, tap_past, tap_now, mixing):
    filter_part, gate_part, hidden, output = saved
    channels = input_traces.shape[-1]
    flat_now = input_traces.reshape(-1, channels)
    flat_past = past_rows.reshape(-1, channels)
    flat_up = incoming_gradient.reshape(-1, channels)
    hidden_grad = jnp.dot(flat_up, mixing.T, preferred_element_type=jnp.float32)
    filter_grad = hidden_grad * gate_part * (1.0 - filter_part * filter_part)
    gate_grad = hidden_grad * filter_part * gate_part * (1.0 - gate_part)
    pre_grad = jnp.concatenate([filter_grad, gate_grad], axis=1).astype(jnp.bfloat16)
    past_term = jnp.einsum("rc,rg->cg", flat_past, pre_grad, preferred_element_type=jnp.float32)
    now_term = jnp.einsum("rc,rg->cg", flat_now, pre_grad, preferred_element_type=jnp.float32)
    mix_term = jnp.einsum("rh,rc->hc", hidden, flat_up, preferred_element_type=jnp.float32)
    ahead_rows = (
        jnp.dot(pre_grad, tap_past.T, preferred_element_type=jnp.float32)
        .astype(jnp.bfloat16)
        .reshape(input_traces.shape)
    )
    local_grad = (
        flat_up.astype(jnp.float32)
        + jnp.dot(pre_grad, tap_now.T, preferred_element_type=jnp.float32)
    ).reshape(input_traces.shape)
    return (local_grad, ahead_rows, (past_term, now_term, mix_term))


def reduce_grads(term_list, scale_factor):
    past_term, now_term, mix_term = term_list
    summed = lax.psum((past_term, now_term, mix_term), ("dp", "tm"))
    return tuple(((member * scale_factor).astype(jnp.bfloat16) for member in summed))


def body(
    signal,
    cotangent,
    first_history_weight,
    first_current_weight,
    first_residual_weight,
    second_history_weight,
    second_current_weight,
    second_residual_weight,
):
    seq_count, number_of_steps, channels = signal.shape
    rows_all = seq_count * lax.axis_size("dp") * number_of_steps * lax.axis_size("tm")
    scale_factor = 1.0 / math.sqrt(rows_all)
    final_rows = signal[:, number_of_steps - FIRST_DILATION :, :]
    received_rows = shifted(final_rows, "tm", 1)
    first_history_rows = jnp.concatenate(
        [received_rows, signal[:, : number_of_steps - FIRST_DILATION, :]], axis=1
    )
    first_layer_stash = forward_layer(
        signal,
        first_history_rows,
        first_history_weight,
        first_current_weight,
        first_residual_weight,
    )
    hidden_activation = first_layer_stash[3]
    distant_offsets = SECOND_DILATION // number_of_steps
    past_two = shifted(hidden_activation, "tm", distant_offsets)
    second_layer_stash = forward_layer(
        hidden_activation,
        past_two,
        second_history_weight,
        second_current_weight,
        second_residual_weight,
    )
    local_two, ahead_two, second_layer_terms = backward_layer(
        hidden_activation,
        past_two,
        second_layer_stash,
        cotangent,
        second_history_weight,
        second_current_weight,
        second_residual_weight,
    )
    arrived_back = shifted(ahead_two, "tm", -distant_offsets)
    hidden_gradient = (local_two + arrived_back.astype(jnp.float32)).astype(jnp.bfloat16)
    reduced_two = reduce_grads(second_layer_terms, scale_factor)
    local_one, forward_rows_first, first_layer_terms = backward_layer(
        signal,
        first_history_rows,
        first_layer_stash,
        hidden_gradient,
        first_history_weight,
        first_current_weight,
        first_residual_weight,
    )
    leading_rows = forward_rows_first[:, :FIRST_DILATION, :]
    received_head_rows = shifted(leading_rows, "tm", -1)
    trailing_later_rows = jnp.concatenate(
        [forward_rows_first[:, FIRST_DILATION:, :], received_head_rows], axis=1
    )
    grad_signal = (local_one + trailing_later_rows.astype(jnp.float32)).astype(jnp.bfloat16)
    reduced_one = reduce_grads(first_layer_terms, scale_factor)
    return (
        grad_signal,
        reduced_one[0],
        reduced_one[1],
        reduced_one[2],
        reduced_two[0],
        reduced_two[1],
        reduced_two[2],
    )


def solution(mesh):
    in_specs = (P("dp", "tm", None), P("dp", "tm", None), P(), P(), P(), P(), P(), P())
    out_specs = (P("dp", "tm", None), P(), P(), P(), P(), P(), P())
    return jax.shard_map(body, mesh=mesh, in_specs=in_specs, out_specs=out_specs, check_vma=False)
```

profile of v0, /device:TPU:2, one launch (start us, length us, event | category | flops | bytes accessed | tf_op | source)
XLA Modules:
  0.0 616.3 jit_solution(2754087225272459337)
XLA Ops:
  7.2 1.1 fusion.28
  8.4 1.9 collective-permute-start
  10.3 1.6 fusion.17
  11.9 11.3 %collective-permute-done = bf16[1,512,256]{2,1,0:T(8,128)(2,1)S(1)} collective-permute-done((bf16[1,512,256]{2,1,0:T(8,128)(2,1)S(1)}, bf16[1,512,256]{2,1,0:T(8,128)(2,1)S(1)}, u32[]{:S(2)}, u32[]{:S(2)}) %collective-permute-start) | collective-permute-done | bytes 262176 | tf_op jit(solution)/shard_map/ppermute | solution.py:14
  24.2 0.6 copy-done.1
  25.2 3.1 collective-permute-start.1
  28.8 23.2 %collective-permute-done.1 = bf16[1,1024,256]{2,1,0:T(8,128)(2,1)S(1)} collective-permute-done((bf16[1,1024,256]{2,1,0:T(8,128)(2,1)S(1)}, bf16[1,1024,256]{2,1,0:T(8,128)(2,1)S(1)}, u32[]{:S(2)}, u32[]{:S(2)}) %collective-permute-start.1) | collective-permute-done | bytes 524320 | tf_op jit(solution)/shard_map/ppermute | solution.py:14
  52.5 0.7 multiply_convert_fusion.4
  53.2 1.3 fusion.26
  55.0 8.9 %collective-permute-start.2 = (bf16[1,1024,256]{2,1,0:T(8,128)(2,1)S(1)}, bf16[1,1024,256]{2,1,0:T(8,128)(2,1)S(1)}, u32[]{:S(2)}, u32[]{:S(2)}) collective-permute-start(bf16[1,1024,256]{2,1,0:T(8,128)(2,1)S(1)} %fusion.2), channel_id=1, source_target_pairs={{8,0},{9,1},{10,2},{11,3},{12,4},{13,5},{14,6},{15,7},{16,8},{17,9... | collective-permute-start | bytes 1572872 | tf_op jit(solution)/shard_map/ppermute | solution.py:14
  64.0 1.3 fusion.13
  65.2 1.3 fusion.12
  66.5 30.5 %collective-permute-done.2 = bf16[1,1024,256]{2,1,0:T(8,128)(2,1)S(1)} collective-permute-done((bf16[1,1024,256]{2,1,0:T(8,128)(2,1)S(1)}, bf16[1,1024,256]{2,1,0:T(8,128)(2,1)S(1)}, u32[]{:S(2)}, u32[]{:S(2)}) %collective-permute-start.2) | collective-permute-done | bytes 524320 | tf_op jit(solution)/shard_map/ppermute | solution.py:14
  97.5 0.7 multiply_convert_fusion.2
  98.2 1.0 fusion.30
  99.2 1.3 convolution_bitcast_fusion
  100.5 1.3 fusion.22
  102.3 13.7 %collective-permute-start.3 = (bf16[1,512,256]{2,1,0:T(8,128)(2,1)S(1)}, bf16[1,512,256]{2,1,0:T(8,128)(2,1)S(1)}, u32[]{:S(2)}, u32[]{:S(2)}) collective-permute-start(bf16[1,512,256]{2,1,0:T(8,128)(2,1)S(1)} %get-tuple-element.18), channel_id=1, source_target_pairs={{1,0},{2,1},{3,2},{4,3},{5,4},{6,5},{7,6},{8,7},{9,8},{10,9},{11,1... | collective-permute-start | bytes 786440 | tf_op jit(solution)/shard_map/ppermute | solution.py:14
  116.1 3.9 collective-permute-done.3
  119.9 1.3 fusion.11
  121.2 483.3 %all-reduce.3.cloned.1.call-done = (f32[256,512]{1,0:T(8,128)}, f32[256,512]{1,0:T(8,128)}, f32[256,256]{1,0:T(8,128)}, f32[256,512]{1,0:T(8,128)}, f32[256,512]{1,0:T(8,128)}, /*index=5*/f32[256,256]{1,0:T(8,128)}) async-done(((f32[256,512]{1,0:T(8,128)}, f32[256,512]{1,0:T(8,128)}, f32[256,256]{1,0:T(8,128)}, f32[256,512]{1,0:T(8,128)}, f32[256,512]{1,0:T(8,128)}, /*index=5*/f32[256,256]{1,0:T(8,128)}), ...) | async-done | bytes 2621456 | tf_op jit(solution)/shard_map/psum | solution.py:61
  604.5 2.2 multiply_convert_fusion.9
  606.7 1.8 multiply_convert_fusion.11
  608.5 0.9 multiply_convert_fusion.7
  (30 shorter events, 3.9 us)
Async XLA Ops:
  7.2 44.8 %copy-start = (bf16[256,512]{1,0:T(8,128)(2,1)S(1)}, bf16[256,512]{1,0:T(8,128)(2,1)}, u32[]{:S(2)}) copy-start(bf16[256,512]{1,0:T(8,128)(2,1)} %param.13) | copy-start | bytes 786436
  7.2 16.1 %copy-start.4 = (bf16[256,512]{1,0:T(8,128)(2,1)S(1)}, bf16[256,512]{1,0:T(8,128)(2,1)}, u32[]{:S(2)}) copy-start(bf16[256,512]{1,0:T(8,128)(2,1)} %param.10) | copy-start | bytes 786436
  7.2 597.3 %all-reduce.3.cloned.1.call-start = ((), (), s32[]{:S(2)}) async-start(), calls=%async_computation | async-start | bytes 5242880 | tf_op jit(solution)/shard_map/psum | solution.py:61
  8.4 14.9 %collective-permute-start = (bf16[1,512,256]{2,1,0:T(8,128)(2,1)S(1)}, bf16[1,512,256]{2,1,0:T(8,128)(2,1)S(1)}, u32[]{:S(2)}, u32[]{:S(2)}) collective-permute-start(bf16[1,512,256]{2,1,0:T(8,128)(2,1)S(1)} %get-tuple-element.19), channel_id=1, source_target_pairs={{0,1},{1,2},{2,3},{3,4},{4,5},{5,6},{6,7},{7,8},{8,9},{9,10},{10,1... | collective-permute-start | bytes 786440 | tf_op jit(solution)/shard_map/ppermute | solution.py:14
  23.7 1.0 copy-start.1
  23.7 1.1 copy-start.7
  23.8 4.5 copy-start.5
  25.2 26.8 %collective-permute-start.1 = (bf16[1,1024,256]{2,1,0:T(8,128)(2,1)S(1)}, bf16[1,1024,256]{2,1,0:T(8,128)(2,1)S(1)}, u32[]{:S(2)}, u32[]{:S(2)}) collective-permute-start(bf16[1,1024,256]{2,1,0:T(8,128)(2,1)S(1)} %bitcast.60), channel_id=1, source_target_pairs={{0,8},{1,9},{2,10},{3,11},{4,12},{5,13},{6,14},{7,15},{8,16},{9,17... | collective-permute-start | bytes 1572872 | tf_op jit(solution)/shard_map/ppermute | solution.py:14
  28.8 23.7 %copy-start.8 = (bf16[1,1024,256]{2,1,0:T(8,128)(2,1)S(1)}, bf16[1,1024,256]{2,1,0:T(8,128)(2,1)}, u32[]{:S(2)}) copy-start(bf16[1,1024,256]{2,1,0:T(8,128)(2,1)} %param.9) | copy-start | bytes 1572868
  28.8 23.7 %copy-start.9 = (bf16[256,256]{1,0:T(8,128)(2,1)S(1)}, bf16[256,256]{1,0:T(8,128)(2,1)}, u32[]{:S(2)}) copy-start(bf16[256,256]{1,0:T(8,128)(2,1)} %param.15) | copy-start | bytes 393220
  55.0 42.0 %collective-permute-start.2 = (bf16[1,1024,256]{2,1,0:T(8,128)(2,1)S(1)}, bf16[1,1024,256]{2,1,0:T(8,128)(2,1)S(1)}, u32[]{:S(2)}, u32[]{:S(2)}) collective-permute-start(bf16[1,1024,256]{2,1,0:T(8,128)(2,1)S(1)} %fusion.2), channel_id=1, source_target_pairs={{8,0},{9,1},{10,2},{11,3},{12,4},{13,5},{14,6},{15,7},{16,8},{17,9... | collective-permute-start | bytes 1572872 | tf_op jit(solution)/shard_map/ppermute | solution.py:14
  101.8 18.2 %copy-start.6 = (bf16[256,512]{1,0:T(8,128)(2,1)S(1)}, bf16[256,512]{1,0:T(8,128)(2,1)}, u32[]{:S(2)}) copy-start(bf16[256,512]{1,0:T(8,128)(2,1)} %param.11) | copy-start | bytes 786436
  102.3 17.6 %collective-permute-start.3 = (bf16[1,512,256]{2,1,0:T(8,128)(2,1)S(1)}, bf16[1,512,256]{2,1,0:T(8,128)(2,1)S(1)}, u32[]{:S(2)}, u32[]{:S(2)}) collective-permute-start(bf16[1,512,256]{2,1,0:T(8,128)(2,1)S(1)} %get-tuple-element.18), channel_id=1, source_target_pairs={{1,0},{2,1},{3,2},{4,3},{5,4},{6,5},{7,6},{8,7},{9,8},{10,9},{11,1... | collective-permute-start | bytes 786440 | tf_op jit(solution)/shard_map/ppermute | solution.py:14
  604.5 4.0 copy-start.2
  604.5 4.0 copy-start.3
Sparse Core Ops, SparseCore 0:
  101.9 502.5 all-reduce.2
where the time goes:
time: 617 us; the launch traced here: 616 us
  waiting for transfers between devices  552 us (89%)
  starting transfers between devices  27.8 us (5%)
  matrix products  14.9 us (2%)
  between operations  14.2 us (2%)
    psum x1, waiting for transfers between devices, reduce_grads(): summed = lax.psum((past_term, now_term, mix_term), ('dp', 'tm'))  483 us
    ppermute x4, waiting for transfers between devices, shifted(): lax.ppermute(value, axis, [(source, source + steps) for source in range(l...  68.9 us
    ppermute x4, starting transfers between devices, shifted(): lax.ppermute(value, axis, [(source, source + steps) for source in range(l...  27.7 us
  transfers between devices with their start and end apart: 5, of which 5 were waited for; matrix products, arithmetic and copies ran while one was open for 1% of the time, Pallas kernels for 0%

commit v1 on v0

--- a/solution.py
+++ b/solution.py
@@ -58,7 +58,8 @@
 
 def reduce_grads(term_list, scale_factor):
     past_term, now_term, mix_term = term_list
-    summed = lax.psum((past_term, now_term, mix_term), ("dp", "tm"))
+    render_circles = lambda obj: lax.psum(lax.psum(obj, "tm"), "dp")
+    summed = render_circles((past_term, now_term, mix_term))
     return tuple(((member * scale_factor).astype(jnp.bfloat16) for member in summed))
 
 

time: 617 us -> 683 us (1.11)
  the two profiles are of different devices: /device:TPU:2 before, /device:TPU:32 now
where the time goes in v1:
time: 683 us; the launch traced here: 682 us
  waiting for transfers between devices  631 us (92%)
  starting transfers between devices  15.5 us (2%)
  matrix products  15 us (2%)
  between operations  14.3 us (2%)
    psum x2, waiting for transfers between devices, reduce_grads(): render_circles = lambda obj: lax.psum(lax.psum(obj, 'tm'), 'dp')  573 us
    ppermute x4, waiting for transfers between devices, shifted(): lax.ppermute(value, axis, [(source, source + steps) for source in range(l...  57.7 us
    ppermute x4, starting transfers between devices, shifted(): lax.ppermute(value, axis, [(source, source + steps) for source in range(l...  15.5 us
  transfers between devices with their start and end apart: 6, of which 6 were waited for; matrix products, arithmetic and copies ran while one was open for 1% of the time, Pallas kernels for 0%

profile of v1, /device:TPU:32, one launch (start us, length us, event | category | flops | bytes accessed | tf_op | source)
XLA Modules:
  0.0 682.4 jit_solution(10499305760429684277)
XLA Ops:
  7.2 1.1 fusion.28
  8.4 1.9 collective-permute-start
  10.3 1.6 fusion.17
  11.9 4.2 collective-permute-done
  18.0 9.1 %collective-permute-start.1 = (bf16[1,1024,256]{2,1,0:T(8,128)(2,1)S(1)}, bf16[1,1024,256]{2,1,0:T(8,128)(2,1)S(1)}, u32[]{:S(2)}, u32[]{:S(2)}) collective-permute-start(bf16[1,1024,256]{2,1,0:T(8,128)(2,1)S(1)} %bitcast.60), channel_id=1, source_target_pairs={{0,8},{1,9},{2,10},{3,11},{4,12},{5,13},{6,14},{7,15},{8,16},{9,17... | collective-permute-start | bytes 1572872 | tf_op jit(solution)/shard_map/ppermute | solution.py:14
  27.6 32.9 %collective-permute-done.1 = bf16[1,1024,256]{2,1,0:T(8,128)(2,1)S(1)} collective-permute-done((bf16[1,1024,256]{2,1,0:T(8,128)(2,1)S(1)}, bf16[1,1024,256]{2,1,0:T(8,128)(2,1)S(1)}, u32[]{:S(2)}, u32[]{:S(2)}) %collective-permute-start.1) | collective-permute-done | bytes 524320 | tf_op jit(solution)/shard_map/ppermute | solution.py:14
  61.1 0.7 multiply_convert_fusion.4
  61.8 1.3 fusion.26
  63.6 1.3 collective-permute-start.2
  64.9 1.3 fusion.13
  66.2 1.3 fusion.12
  67.4 16.8 %collective-permute-done.2 = bf16[1,1024,256]{2,1,0:T(8,128)(2,1)S(1)} collective-permute-done((bf16[1,1024,256]{2,1,0:T(8,128)(2,1)S(1)}, bf16[1,1024,256]{2,1,0:T(8,128)(2,1)S(1)}, u32[]{:S(2)}, u32[]{:S(2)}) %collective-permute-start.2) | collective-permute-done | bytes 524320 | tf_op jit(solution)/shard_map/ppermute | solution.py:14
  84.7 0.7 multiply_convert_fusion.2
  85.4 1.0 fusion.30
  86.4 1.3 convolution_bitcast_fusion
  87.7 1.3 fusion.22
  89.0 471.6 %all-reduce.5.cloned.1.call-done = (f32[256,512]{1,0:T(8,128)}, f32[256,512]{1,0:T(8,128)}, f32[256,256]{1,0:T(8,128)}, f32[256,512]{1,0:T(8,128)}, f32[256,512]{1,0:T(8,128)}, /*index=5*/f32[256,256]{1,0:T(8,128)}) async-done(((f32[256,512]{1,0:T(8,128)}, f32[256,512]{1,0:T(8,128)}, f32[256,256]{1,0:T(8,128)}, f32[256,512]{1,0:T(8,128)}, f32[256,512]{1,0:T(8,128)}, /*index=5*/f32[256,256]{1,0:T(8,128)}), ...) | async-done | bytes 2621456 | tf_op jit(solution)/shard_map/psum | solution.py:61
  561.2 3.1 collective-permute-start.3
  564.3 3.9 collective-permute-done.3
  568.2 1.3 fusion.11
  569.5 101.2 %all-reduce.7.cloned.1.call-done = (f32[256,512]{1,0:T(8,128)}, f32[256,512]{1,0:T(8,128)}, f32[256,256]{1,0:T(8,128)}, f32[256,512]{1,0:T(8,128)}, f32[256,512]{1,0:T(8,128)}, /*index=5*/f32[256,256]{1,0:T(8,128)}) async-done(((f32[256,512]{1,0:T(8,128)}, f32[256,512]{1,0:T(8,128)}, f32[256,256]{1,0:T(8,128)}, f32[256,512]{1,0:T(8,128)}, f32[256,512]{1,0:T(8,128)}, /*index=5*/f32[256,256]{1,0:T(8,128)}), ...) | async-done | bytes 2621456 | tf_op jit(solution)/shard_map/psum | solution.py:61
  670.7 2.2 multiply_convert_fusion.9
  672.9 1.8 multiply_convert_fusion.11
  674.7 0.9 multiply_convert_fusion.7
  (33 shorter events, 4.5 us)
Async XLA Ops:
  7.2 53.4 %copy-start = (bf16[256,512]{1,0:T(8,128)(2,1)S(1)}, bf16[256,512]{1,0:T(8,128)(2,1)}, u32[]{:S(2)}) copy-start(bf16[256,512]{1,0:T(8,128)(2,1)} %param.13) | copy-start | bytes 786436
  7.2 8.9 %copy-start.4 = (bf16[256,512]{1,0:T(8,128)(2,1)S(1)}, bf16[256,512]{1,0:T(8,128)(2,1)}, u32[]{:S(2)}) copy-start(bf16[256,512]{1,0:T(8,128)(2,1)} %param.10) | copy-start | bytes 786436
  7.2 553.5 %all-reduce.5.cloned.1.call-start = ((), (), s32[]{:S(2)}) async-start(), calls=%async_computation | async-start | bytes 5242880 | tf_op jit(solution)/shard_map/psum | solution.py:61
  8.4 7.7 %collective-permute-start = (bf16[1,512,256]{2,1,0:T(8,128)(2,1)S(1)}, bf16[1,512,256]{2,1,0:T(8,128)(2,1)S(1)}, u32[]{:S(2)}, u32[]{:S(2)}) collective-permute-start(bf16[1,512,256]{2,1,0:T(8,128)(2,1)S(1)} %get-tuple-element.25), channel_id=1, source_target_pairs={{0,1},{1,2},{2,3},{3,4},{4,5},{5,6},{6,7},{7,8},{8,9},{9,10},{10,1... | collective-permute-start | bytes 786440 | tf_op jit(solution)/shard_map/ppermute | solution.py:14
  16.6 1.0 copy-start.1
  16.6 1.1 copy-start.7
  16.6 10.5 %copy-start.5 = (bf16[256,512]{1,0:T(8,128)(2,1)S(1)}, bf16[256,512]{1,0:T(8,128)(2,1)}, u32[]{:S(2)}) copy-start(bf16[256,512]{1,0:T(8,128)(2,1)} %param.14) | copy-start | bytes 786436
  18.0 42.6 %collective-permute-start.1 = (bf16[1,1024,256]{2,1,0:T(8,128)(2,1)S(1)}, bf16[1,1024,256]{2,1,0:T(8,128)(2,1)S(1)}, u32[]{:S(2)}, u32[]{:S(2)}) collective-permute-start(bf16[1,1024,256]{2,1,0:T(8,128)(2,1)S(1)} %bitcast.60), channel_id=1, source_target_pairs={{0,8},{1,9},{2,10},{3,11},{4,12},{5,13},{6,14},{7,15},{8,16},{9,17... | collective-permute-start | bytes 1572872 | tf_op jit(solution)/shard_map/ppermute | solution.py:14
  27.6 33.5 %copy-start.8 = (bf16[1,1024,256]{2,1,0:T(8,128)(2,1)S(1)}, bf16[1,1024,256]{2,1,0:T(8,128)(2,1)}, u32[]{:S(2)}) copy-start(bf16[1,1024,256]{2,1,0:T(8,128)(2,1)} %param.9) | copy-start | bytes 1572868
  27.6 33.5 %copy-start.9 = (bf16[256,256]{1,0:T(8,128)(2,1)S(1)}, bf16[256,256]{1,0:T(8,128)(2,1)}, u32[]{:S(2)}) copy-start(bf16[256,256]{1,0:T(8,128)(2,1)} %param.15) | copy-start | bytes 393220
  63.6 20.6 %collective-permute-start.2 = (bf16[1,1024,256]{2,1,0:T(8,128)(2,1)S(1)}, bf16[1,1024,256]{2,1,0:T(8,128)(2,1)S(1)}, u32[]{:S(2)}, u32[]{:S(2)}) collective-permute-start(bf16[1,1024,256]{2,1,0:T(8,128)(2,1)S(1)} %fusion.2), channel_id=1, source_target_pairs={{8,0},{9,1},{10,2},{11,3},{12,4},{13,5},{14,6},{15,7},{16,8},{17,9... | collective-permute-start | bytes 1572872 | tf_op jit(solution)/shard_map/ppermute | solution.py:14
  89.0 581.7 %all-reduce.7.cloned.1.call-start = ((), (), s32[]{:S(2)}) async-start(), calls=%async_computation.1 | async-start | bytes 5242880 | tf_op jit(solution)/shard_map/psum | solution.py:61
  560.7 7.5 %copy-start.6 = (bf16[256,512]{1,0:T(8,128)(2,1)S(1)}, bf16[256,512]{1,0:T(8,128)(2,1)}, u32[]{:S(2)}) copy-start(bf16[256,512]{1,0:T(8,128)(2,1)} %param.11) | copy-start | bytes 786436
  561.2 7.0 %collective-permute-start.3 = (bf16[1,512,256]{2,1,0:T(8,128)(2,1)S(1)}, bf16[1,512,256]{2,1,0:T(8,128)(2,1)S(1)}, u32[]{:S(2)}, u32[]{:S(2)}) collective-permute-start(bf16[1,512,256]{2,1,0:T(8,128)(2,1)S(1)} %get-tuple-element.24), channel_id=1, source_target_pairs={{1,0},{2,1},{3,2},{4,3},{5,4},{6,5},{7,6},{8,7},{9,8},{10,9},{11,1... | collective-permute-start | bytes 786440 | tf_op jit(solution)/shard_map/ppermute | solution.py:14
  670.7 4.0 copy-start.2
  670.7 4.0 copy-start.3
Sparse Core Ops, SparseCore 0:
  89.1 471.4 all-reduce.4
  564.4 106.2 all-reduce.6
